TPU v7x, 32 devices: a whole 2x2x4 slice. The times are simulated.
32 devices in a mesh: grp: 4 (over x, core), ep: 8 (over z, y).
Axes of the slice: x: 2, y: 2, z: 4, core: 2. Of those that a mesh axis runs over, the one named last changes fastest.
Arguments:
- tokens: bfloat16 [2048, 5120], P('ep', 'grp'), may hold values from -6 to 6
- cotangent: bfloat16 [2048, 5120], P('ep', 'grp'), may hold values from -0.59765625 to 0.59765625
- gate_weights: bfloat16 [2048, 6], P('ep'), may hold values from 0.099609375 to 1
- expert_ids: int32 [2048, 6], P('ep'), may hold values from 0 to 159, all different within a row; in each aligned block of 256 rows (0 to 255, 256 to 511, ...) at most 16 rows name the same one
- hot_ids: int32 [2], replicated, may hold values from 8 to 159, as said below
- gate_cold: bfloat16 [8, 5120, 768], P('ep', 'grp'), may hold values from -0.078125 to 0.078125
- up_cold: bfloat16 [8, 5120, 768], P('ep', 'grp'), may hold values from -0.078125 to 0.078125
- down_cold: bfloat16 [8, 768, 5120], P('ep', None, 'grp'), may hold values from -0.21875 to 0.21875
- gate_hot: bfloat16 [2, 5120, 768], P(None, 'grp', 'ep'), may hold values from -0.078125 to 0.078125
- up_hot: bfloat16 [2, 5120, 768], P(None, 'grp', 'ep'), may hold values from -0.078125 to 0.078125
- down_hot: bfloat16 [2, 768, 5120], P(None, 'ep', 'grp'), may hold values from -0.21875 to 0.21875
Outputs:
- grad_gate_cold: bfloat16 [8, 5120, 768], P('ep', 'grp')
- grad_up_cold: bfloat16 [8, 5120, 768], P('ep', 'grp')
- grad_down_cold: bfloat16 [8, 768, 5120], P('ep', None, 'grp')
- grad_gate_hot: float32 [2, 5120, 768], P(None, 'grp', 'ep')
- grad_up_hot: float32 [2, 5120, 768], P(None, 'grp', 'ep')
- grad_down_hot: float32 [2, 768, 5120], P(None, 'ep', 'grp')
- gate_weight_grad: float32 [2048, 6], P('ep')
Inputs may be any that keep to these rules, and one draw needn't show every extreme that they name: `expert_ids`: each row names 6 different experts. Among the routes of the 256 tokens of one index of ep (aligned blocks of rows) no expert is named more than 16 times, a bound that some block reaches. `hot_ids`: distinct expert numbers, none below 8; expert 160 - 1 is always among them.
All inputs are finite; a program needn't handle non-finite values.
Results may differ from a plain program's by a relative error of at most 0.02.
Values may be sent and summed in bfloat16 or wider, within the bound.
No kernel may reach another device: no remote copies, remote signals or barrier semaphores. Data moves between devices by JAX's collectives and lax.ppermute only.
A program may use at most 128 MiB of HBM per device.

v0:
```python
import jax
import jax.numpy as jnp
from jax import lax
from jax.sharding import PartitionSpec as P


def route_table(flat_ids, targets, capacity):
    matches = (flat_ids[:, None] == targets[None, :]).astype(jnp.int32)
    rank_of = jnp.cumsum(matches, axis=0) - 1
    slot_of = jnp.sum(matches * rank_of, axis=1)
    owner_of = jnp.sum(matches * jnp.arange(targets.shape[0], dtype=jnp.int32)[None, :], axis=1)
    usable = jnp.sum(matches, axis=1) > 0
    row_of = owner_of * capacity + slot_of
    rows_total = targets.shape[0] * capacity
    route_map = (row_of[None, :] == jnp.arange(rows_total, dtype=jnp.int32)[:, None]) & usable[
        None, :
    ]
    return route_map.astype(jnp.float32)


def gather_rows(route_map, tokens, cotangent, flat_weights, tok_rows, top_count):
    per_token = jnp.sum(route_map.reshape(route_map.shape[0], tok_rows, top_count), axis=2)
    token_map = per_token.astype(jnp.bfloat16)
    feat_rows = jnp.dot(token_map, tokens, preferred_element_type=jnp.float32).astype(jnp.bfloat16)
    cotan_rows = jnp.dot(token_map, cotangent, preferred_element_type=jnp.float32).astype(
        jnp.bfloat16
    )
    scale_rows = jnp.dot(
        route_map, flat_weights.astype(jnp.float32), precision=lax.Precision.HIGHEST
    )
    return (feat_rows, cotan_rows, scale_rows.astype(jnp.bfloat16))


def swiglu_back(pre_gate, pre_up, grad_hidden):
    sigmoid_gate = jax.nn.sigmoid(pre_gate)
    activated = pre_gate * sigmoid_gate
    hidden = (activated * pre_up).astype(jnp.bfloat16)
    back_gate = (
        grad_hidden * pre_up * sigmoid_gate * (1.0 + pre_gate * (1.0 - sigmoid_gate))
    ).astype(jnp.bfloat16)
    back_up = (grad_hidden * activated).astype(jnp.bfloat16)
    return (hidden, back_gate, back_up)


def body(
    tokens,
    cotangent,
    gate_weights,
    expert_ids,
    hot_ids,
    gate_cold,
    up_cold,
    down_cold,
    gate_hot,
    up_hot,
    down_hot,
):
    tok_rows, slice_width = tokens.shape
    top_count = expert_ids.shape[1]
    cold_count = lax.axis_size("ep")
    hot_count = hot_ids.shape[0]
    capacity = tok_rows // 16
    flat_ids = expert_ids.reshape(-1)
    flat_weights = gate_weights.reshape(-1)
    cold_map = route_table(flat_ids, jnp.arange(cold_count, dtype=jnp.int32), capacity)
    hot_map = route_table(flat_ids, hot_ids, capacity)
    cold_feats, cold_cotan, cold_scale = gather_rows(
        cold_map, tokens, cotangent, flat_weights, tok_rows, top_count
    )
    hot_feats, hot_cotan, hot_scale = gather_rows(
        hot_map, tokens, cotangent, flat_weights, tok_rows, top_count
    )
    outgoing = (
        cold_feats.reshape(cold_count, capacity, slice_width),
        cold_cotan.reshape(cold_count, capacity, slice_width),
        cold_scale.reshape(cold_count, capacity),
    )
    recv_feats, recv_cotan, recv_scale = (
        lax.all_to_all(outgoing[0], "ep", split_axis=0, concat_axis=0, tiled=True),
        lax.all_to_all(outgoing[1], "ep", split_axis=0, concat_axis=0, tiled=True),
        lax.all_to_all(outgoing[2], "ep", split_axis=0, concat_axis=0, tiled=True),
    )
    recv_feats = recv_feats.reshape(-1, slice_width)
    recv_cotan = recv_cotan.reshape(-1, slice_width)
    weighted = (
        recv_scale.reshape(-1).astype(jnp.float32)[:, None] * recv_cotan.astype(jnp.float32)
    ).astype(jnp.bfloat16)
    w_gate = gate_cold[0]
    w_up = up_cold[0]
    w_down = down_cold[0]
    part_gate = jnp.dot(recv_feats, w_gate, preferred_element_type=jnp.float32)
    part_up = jnp.dot(recv_feats, w_up, preferred_element_type=jnp.float32)
    part_hidden = lax.dot_general(
        weighted, w_down, (((1,), (1,)), ((), ())), preferred_element_type=jnp.float32
    )
    pre_gate, pre_up, grad_hidden = (
        lax.psum(part_gate.astype(jnp.bfloat16), "grp").astype(jnp.float32),
        lax.psum(part_up.astype(jnp.bfloat16), "grp").astype(jnp.float32),
        lax.psum(part_hidden.astype(jnp.bfloat16), "grp").astype(jnp.float32),
    )
    hidden, back_gate, back_up = swiglu_back(pre_gate, pre_up, grad_hidden)
    output_slice = jnp.dot(hidden, w_down, preferred_element_type=jnp.float32)
    cold_route = jnp.sum(output_slice * recv_cotan.astype(jnp.float32), axis=1)
    contract_rows = (((0,), (0,)), ((), ()))
    grad_gate_cold = lax.dot_general(
        recv_feats, back_gate, contract_rows, preferred_element_type=jnp.float32
    )
    grad_up_cold = lax.dot_general(
        recv_feats, back_up, contract_rows, preferred_element_type=jnp.float32
    )
    grad_down_cold = lax.dot_general(
        hidden, weighted, contract_rows, preferred_element_type=jnp.float32
    )
    hot_feats = hot_feats.reshape(hot_count, capacity, slice_width)
    hot_cotan = hot_cotan.reshape(hot_count, capacity, slice_width)
    hot_scale = hot_scale.reshape(hot_count, capacity)
    full_gate, full_up = (
        lax.all_gather(gate_hot, "ep", axis=2, tiled=True),
        lax.all_gather(up_hot, "ep", axis=2, tiled=True),
    )
    full_down = lax.all_gather(down_hot, "ep", axis=1, tiled=True)
    hot_weighted = (
        hot_scale.astype(jnp.float32)[:, :, None] * hot_cotan.astype(jnp.float32)
    ).astype(jnp.bfloat16)
    part_gate_hot = jnp.einsum(
        "jcd,jdh->jch", hot_feats, full_gate, preferred_element_type=jnp.float32
    )
    part_up_hot = jnp.einsum("jcd,jdh->jch", hot_feats, full_up, preferred_element_type=jnp.float32)
    part_hidden_hot = jnp.einsum(
        "jcd,jhd->jch", hot_weighted, full_down, preferred_element_type=jnp.float32
    )
    pre_gate_hot, pre_up_hot, grad_hidden_hot = (
        lax.psum(part_gate_hot.astype(jnp.bfloat16), "grp").astype(jnp.float32),
        lax.psum(part_up_hot.astype(jnp.bfloat16), "grp").astype(jnp.float32),
        lax.psum(part_hidden_hot.astype(jnp.bfloat16), "grp").astype(jnp.float32),
    )
    hidden_hot, back_gate_hot, back_up_hot = swiglu_back(pre_gate_hot, pre_up_hot, grad_hidden_hot)
    output_hot = jnp.einsum(
        "jch,jhd->jcd", hidden_hot, full_down, preferred_element_type=jnp.float32
    )
    hot_route_part = jnp.sum(output_hot * hot_cotan.astype(jnp.float32), axis=2)
    shadow_gate = jnp.einsum(
        "jcd,jch->jdh", hot_feats, back_gate_hot, preferred_element_type=jnp.float32
    )
    shadow_up = jnp.einsum(
        "jcd,jch->jdh", hot_feats, back_up_hot, preferred_element_type=jnp.float32
    )
    shadow_down = jnp.einsum(
        "jch,jcd->jdh", hidden_hot, hot_weighted, preferred_element_type=jnp.float32
    )
    grad_gate_hot, grad_up_hot, down_turned = (
        lax.psum_scatter(
            shadow_gate.astype(jnp.bfloat16), "ep", scatter_dimension=2, tiled=True
        ).astype(jnp.float32),
        lax.psum_scatter(
            shadow_up.astype(jnp.bfloat16), "ep", scatter_dimension=2, tiled=True
        ).astype(jnp.float32),
        lax.psum_scatter(
            shadow_down.astype(jnp.bfloat16), "ep", scatter_dimension=2, tiled=True
        ).astype(jnp.float32),
    )
    grad_down_hot = jnp.transpose(down_turned, (0, 2, 1))
    cold_route, hot_route = lax.psum((cold_route, hot_route_part), "grp")
    cold_back = lax.all_to_all(
        cold_route.reshape(cold_count, capacity), "ep", split_axis=0, concat_axis=0, tiled=True
    )
    route_flat = jnp.dot(cold_back.reshape(-1), cold_map, precision=lax.Precision.HIGHEST)
    route_flat = route_flat + jnp.dot(
        hot_route.reshape(-1), hot_map, precision=lax.Precision.HIGHEST
    )
    gate_weight_grad = route_flat.reshape(tok_rows, top_count)
    return (
        grad_gate_cold[None].astype(jnp.bfloat16),
        grad_up_cold[None].astype(jnp.bfloat16),
        grad_down_cold[None].astype(jnp.bfloat16),
        grad_gate_hot,
        grad_up_hot,
        grad_down_hot,
        gate_weight_grad,
    )


def solution(mesh):
    in_specs = (
        P("ep", "grp"),
        P("ep", "grp"),
        P("ep", None),
        P("ep", None),
        P(),
        P("ep", "grp", None),
        P("ep", "grp", None),
        P("ep", None, "grp"),
        P(None, "grp", "ep"),
        P(None, "grp", "ep"),
        P(None, "ep", "grp"),
    )
    out_specs = (
        P("ep", "grp", None),
        P("ep", "grp", None),
        P("ep", None, "grp"),
        P(None, "grp", "ep"),
        P(None, "grp", "ep"),
        P(None, "ep", "grp"),
        P("ep", None),
    )
    return jax.shard_map(body, mesh=mesh, in_specs=in_specs, out_specs=out_specs, check_vma=False)
```

profile of v0, /device:TPU:0, one launch (start us, length us, event | category | flops | bytes accessed | tf_op | source)
XLA Modules:
  0.0 574.7 jit_solution(6589414462695450256)
XLA Ops:
  17.9 7.3 %all-to-all-start.1 = ((bf16[8,1,16]{2,1,0:T(2,128)(2,1)}), bf16[8,1,16]{2,1,0:T(2,128)(2,1)S(1)}, u32[]{:S(2)}, u32[]{:S(2)}) async-start(bf16[8,1,16]{2,1,0:T(2,128)(2,1)} %all_to_all.24), calls=%async_computation.1 | async-start | bytes 8192 | tf_op jit(solution)/shard_map/all_to_all | solution.py:81
  33.5 6.0 %all-to-all-start = ((bf16[8,16,1280]{2,1,0:T(8,128)(2,1)}), bf16[8,16,1280]{2,1,0:T(8,128)(2,1)S(1)}, u32[]{:S(2)}, u32[]{:S(2)}) async-start(bf16[8,16,1280]{2,1,0:T(8,128)(2,1)} %bitcast.121), calls=%async_computation | async-start | bytes 655360 | tf_op jit(solution)/shard_map/all_to_all | solution.py:79
  40.7 11.0 %all-to-all-done = bf16[8,16,1280]{2,1,0:T(8,128)(2,1)S(1)} async-done(((bf16[8,16,1280]{2,1,0:T(8,128)(2,1)}), bf16[8,16,1280]{2,1,0:T(8,128)(2,1)S(1)}, u32[]{:S(2)}, u32[]{:S(2)}) %all-to-all-start) | async-done | bytes 327712 | tf_op jit(solution)/shard_map/all_to_all | solution.py:79
  51.8 5.0 all-to-all-start.2
  56.8 2.7 fusion.16
  62.1 13.3 %all-to-all-done.2 = bf16[8,16,1280]{2,1,0:T(8,128)(2,1)S(1)} async-done(((bf16[8,16,1280]{2,1,0:T(8,128)(2,1)}), bf16[8,16,1280]{2,1,0:T(8,128)(2,1)S(1)}, u32[]{:S(2)}, u32[]{:S(2)}) %all-to-all-start.2) | async-done | bytes 327712 | tf_op jit(solution)/shard_map/all_to_all | solution.py:80
  75.5 12.9 %all-gather.8.cloned.1.call-done = bf16[2,1280,768]{1,2,0:T(8,128)(2,1)} async-done(((bf16[2,1280,96]{1,2,0:T(8,128)(2,1)}), bf16[2,1280,768]{1,2,0:T(8,128)(2,1)}) %all-gather.8.cloned.1.call-update) | async-done | bytes 3932176 | tf_op jit(solution)/shard_map/all_gather | solution.py:118
  88.4 3.9 convolution_convert_fusion.10
  92.3 67.5 %all-gather.6.cloned.1.call-done = bf16[2,1280,768]{1,2,0:T(8,128)(2,1)} async-done(((bf16[2,1280,96]{1,2,0:T(8,128)(2,1)}), bf16[2,1280,768]{1,2,0:T(8,128)(2,1)}) %all-gather.6.cloned.1.call-update) | async-done | bytes 3932176 | tf_op jit(solution)/shard_map/all_gather | solution.py:119
  159.7 3.9 convolution_convert_fusion.11
  163.6 66.8 %all-gather.4.cloned.1.call-done = bf16[2,768,1280]{2,1,0:T(8,128)(2,1)} async-done(((bf16[2,96,1280]{2,1,0:T(8,128)(2,1)}), bf16[2,768,1280]{2,1,0:T(8,128)(2,1)}) %all-gather.4.cloned.1.call-update) | async-done | bytes 3932176 | tf_op jit(solution)/shard_map/all_gather | solution.py:121
  230.4 3.9 convolution_convert_fusion.12
  235.9 27.8 %all-reduce.6.cloned.1.call-done = (bf16[2,16,768]{2,1,0:T(8,128)(2,1)}, bf16[2,16,768]{2,1,0:T(8,128)(2,1)}, bf16[2,16,768]{2,1,0:T(8,128)(2,1)}) async-done(((bf16[2,16,768]{2,1,0:T(8,128)(2,1)}, bf16[2,16,768]{2,1,0:T(8,128)(2,1)}, bf16[2,16,768]{2,1,0:T(8,128)(2,1)}), (bf16[2,16,768]{2,1,0:T(8,128)(2,1)}, bf16[2,16,768]{2,1,0:T(8,128)(2,1)}, bf16[2,16,768]{2,1,0:T(8,128)(2,1)})) %all-reduce.6.cloned.1.call-update) | async-done | bytes 147472 | tf_op jit(solution)/shard_map/psum | solution.py:134
  263.8 4.0 convolution_convert_fusion.1
  267.9 3.2 convolution_convert_fusion
  271.4 3.2 convolution_convert_fusion.2
  274.8 26.7 %all-reduce.8.cloned.1.call-done = (bf16[128,768]{1,0:T(8,128)(2,1)}, bf16[128,768]{1,0:T(8,128)(2,1)}, bf16[128,768]{1,0:T(8,128)(2,1)}) async-done(((bf16[128,768]{1,0:T(8,128)(2,1)}, bf16[128,768]{1,0:T(8,128)(2,1)}, bf16[128,768]{1,0:T(8,128)(2,1)}), (bf16[128,768]{1,0:T(8,128)(2,1)}, bf16[128,768]{1,0:T(8,128)(2,1)}, bf16[128,768]{1,0:T(8,128)(2,1)})) %all-reduce.8.cloned.1.call-update) | async-done | bytes 589840 | tf_op jit(solution)/shard_map/psum | solution.py:98
  305.3 2.9 fusion.1
  311.0 6.4 %all-reduce = (f32[8,1,16]{2,0,1:T(8,128)}, f32[32]{0:T(128)S(1)}) all-reduce(f32[8,1,16]{2,0,1:T(8,128)S(1)} %all_to_all.22, f32[32]{0:T(128)S(1)} %reshape.191), channel_id=1, replica_groups=mesh['grp'=4,'ep'=8] {'grp'}, use_global_device_ids=true, to_apply=%region_22.23 | all-reduce | flops 160 | bytes 1280 | tf_op jit(solution)/shard_map/psum | solution.py:163
  317.4 5.8 %all-to-all-start.3 = ((f32[8,1,16]{2,1,0:T(1,128)}), f32[8,1,16]{2,1,0:T(1,128)S(1)}, u32[]{:S(2)}, u32[]{:S(2)}) async-start(f32[8,1,16]{2,1,0:T(1,128)} %bitcast.19), calls=%async_computation.6 | async-start | bytes 8192 | tf_op jit(solution)/shard_map/all_to_all | solution.py:164
  323.5 6.4 %all-to-all-done.3 = f32[8,1,16]{2,1,0:T(1,128)S(1)} async-done(((f32[8,1,16]{2,1,0:T(1,128)}), f32[8,1,16]{2,1,0:T(1,128)S(1)}, u32[]{:S(2)}, u32[]{:S(2)}) %all-to-all-start.3) | async-done | bytes 544 | tf_op jit(solution)/shard_map/all_to_all | solution.py:164
  332.4 57.6 %reduce-scatter.6.cloned.1.call-done = bf16[2,1280,96]{1,2,0:T(8,128)(2,1)} async-done(((bf16[2,1280,768]{1,2,0:T(8,128)(2,1)}), bf16[2,1280,96]{1,2,0:T(8,128)(2,1)}) %reduce-scatter.6.cloned.1.call-update) | async-done | bytes 491536 | tf_op jit(solution)/shard_map/reduce_scatter | solution.py:155
  392.0 85.7 %reduce-scatter.8.cloned.1.call-done = bf16[2,1280,96]{1,2,0:T(8,128)(2,1)} async-done(((bf16[2,1280,768]{1,2,0:T(8,128)(2,1)}), bf16[2,1280,96]{1,2,0:T(8,128)(2,1)}) %reduce-scatter.8.cloned.1.call-update) | async-done | bytes 491536 | tf_op jit(solution)/shard_map/reduce_scatter | solution.py:158
  479.7 86.1 %reduce-scatter.4.cloned.1.call-done = bf16[2,1280,96]{1,2,0:T(8,128)(2,1)} async-done(((bf16[2,1280,768]{1,2,0:T(8,128)(2,1)}), bf16[2,1280,96]{1,2,0:T(8,128)(2,1)}) %reduce-scatter.4.cloned.1.call-update) | async-done | bytes 491536 | tf_op jit(solution)/shard_map/reduce_scatter | solution.py:152
  (99 shorter events, 40.3 us)
Async XLA Ops:
  7.2 227.2 %copy-start = (bf16[1,768,1280]{2,1,0:T(8,128)(2,1)S(1)}, bf16[1,768,1280]{2,1,0:T(8,128)(2,1)}, u32[]{:S(2)}) copy-start(bf16[1,768,1280]{2,1,0:T(8,128)(2,1)} %param.18) | copy-start | bytes 5898244
  7.2 24.8 %copy-start.2 = (bf16[256,1280]{1,0:T(8,128)(2,1)S(1)}, bf16[256,1280]{1,0:T(8,128)(2,1)}, u32[]{:S(2)}) copy-start(bf16[256,1280]{1,0:T(8,128)(2,1)} %param.11) | copy-start | bytes 1966084
  7.2 26.1 %copy-start.3 = (bf16[256,1280]{1,0:T(8,128)(2,1)S(1)}, bf16[256,1280]{1,0:T(8,128)(2,1)}, u32[]{:S(2)}) copy-start(bf16[256,1280]{1,0:T(8,128)(2,1)} %param.12) | copy-start | bytes 1966084
  7.2 81.2 %all-gather.8.cloned.1.call-start = ((), (), s32[]{:S(2)}) async-start(), calls=%async_computation.9 | async-start | bytes 4423680 | tf_op jit(solution)/shard_map/all_gather | solution.py:118
  7.9 151.8 %all-gather.6.cloned.1.call-start = ((), (), s32[]{:S(2)}) async-start(), calls=%async_computation.8 | async-start | bytes 4423680 | tf_op jit(solution)/shard_map/all_gather | solution.py:119
  8.7 221.7 %all-gather.4.cloned.1.call-start = ((), (), s32[]{:S(2)}) async-start(), calls=%async_computation.7 | async-start | bytes 4423680 | tf_op jit(solution)/shard_map/all_gather | solution.py:121
  17.9 15.6 %all-to-all-start.1 = ((bf16[8,1,16]{2,1,0:T(2,128)(2,1)}), bf16[8,1,16]{2,1,0:T(2,128)(2,1)S(1)}, u32[]{:S(2)}, u32[]{:S(2)}) async-start(bf16[8,1,16]{2,1,0:T(2,128)(2,1)} %all_to_all.24), calls=%async_computation.1 | async-start | bytes 8192 | tf_op jit(solution)/shard_map/all_to_all | solution.py:81
  33.5 18.3 %all-to-all-start = ((bf16[8,16,1280]{2,1,0:T(8,128)(2,1)}), bf16[8,16,1280]{2,1,0:T(8,128)(2,1)S(1)}, u32[]{:S(2)}, u32[]{:S(2)}) async-start(bf16[8,16,1280]{2,1,0:T(8,128)(2,1)} %bitcast.121), calls=%async_computation | async-start | bytes 655360 | tf_op jit(solution)/shard_map/all_to_all | solution.py:79
  51.8 23.6 %all-to-all-start.2 = ((bf16[8,16,1280]{2,1,0:T(8,128)(2,1)}), bf16[8,16,1280]{2,1,0:T(8,128)(2,1)S(1)}, u32[]{:S(2)}, u32[]{:S(2)}) async-start(bf16[8,16,1280]{2,1,0:T(8,128)(2,1)} %bitcast.122), calls=%async_computation.2 | async-start | bytes 655360 | tf_op jit(solution)/shard_map/all_to_all | solution.py:80
  56.7 207.0 %all-reduce.6.cloned.1.call-start = ((), (), s32[]{:S(2)}) async-start(), calls=%async_computation.13 | async-start | bytes 294912 | tf_op jit(solution)/shard_map/psum | solution.py:134
  234.3 67.2 %all-reduce.8.cloned.1.call-start = ((), (), s32[]{:S(2)}) async-start(), calls=%async_computation.14 | async-start | bytes 1179648 | tf_op jit(solution)/shard_map/psum | solution.py:98
  235.9 154.1 %reduce-scatter.6.cloned.1.call-start = ((), (), s32[]{:S(2)}) async-start(), calls=%async_computation.11 | async-start | bytes 4423680 | tf_op jit(solution)/shard_map/reduce_scatter | solution.py:155
  263.7 4.1 copy-start.5
  263.7 4.1 copy-start.6
  267.8 209.9 %reduce-scatter.8.cloned.1.call-start = ((), (), s32[]{:S(2)}) async-start(), calls=%async_computation.12 | async-start | bytes 4423680 | tf_op jit(solution)/shard_map/reduce_scatter | solution.py:158
  267.9 3.5 copy-start.9
  271.1 294.7 %reduce-scatter.4.cloned.1.call-start = ((), (), s32[]{:S(2)}) async-start(), calls=%async_computation.10 | async-start | bytes 4423680 | tf_op jit(solution)/shard_map/reduce_scatter | solution.py:152
  301.5 1.7 copy-start.4
  301.5 1.7 copy-start.7
  303.2 5.0 copy-start.8
  303.3 7.0 %copy-start.1 = (bf16[2,768,1280]{2,1,0:T(8,128)(2,1)S(1)}, bf16[2,768,1280]{2,1,0:T(8,128)(2,1)}, u32[]{:S(2)}) copy-start(bf16[2,768,1280]{2,1,0:T(8,128)(2,1)} %all-gather.4.cloned.1.call-done) | copy-start | bytes 11796484
  317.4 12.4 %all-to-all-start.3 = ((f32[8,1,16]{2,1,0:T(1,128)}), f32[8,1,16]{2,1,0:T(1,128)S(1)}, u32[]{:S(2)}, u32[]{:S(2)}) async-start(f32[8,1,16]{2,1,0:T(1,128)} %bitcast.19), calls=%async_computation.6 | async-start | bytes 8192 | tf_op jit(solution)/shard_map/all_to_all | solution.py:164
Sparse Core Ops, SparseCore 0:
  10.2 78.1 all-gather.7
  90.6 69.1 all-gather.5
  161.9 68.4 all-gather.3
  234.4 29.2 all-reduce.5
  266.9 34.6 all-reduce.7
  305.5 84.4 reduce-scatter.5
  393.7 83.9 reduce-scatter.7
  481.8 83.9 reduce-scatter.3
where the time goes:
time: 576 us; the launch traced here: 575 us
  waiting for transfers between devices  464 us (81%)
  matrix products  41.6 us (7%)
  starting transfers between devices  24.6 us (4%)
  between operations  14.4 us (2%)
  other arithmetic  12.2 us (2%)
  local copies, waits for them, and re-layouts  11.6 us (2%)
  blocking collectives  6.41 us (1%)
    reduce_scatter x1, waiting for transfers between devices, body(): lax.psum_scatter(shadow_gate.astype(jnp.bfloat16), 'ep', scatter_dimensio...  86.1 us
    reduce_scatter x1, waiting for transfers between devices, body(): lax.psum_scatter(shadow_down.astype(jnp.bfloat16), 'ep', scatter_dimensio...  85.7 us
    all_gather x1, waiting for transfers between devices, body(): lax.all_gather(up_hot, 'ep', axis=2, tiled=True)  67.5 us
    all_gather x1, waiting for transfers between devices, body(): full_down = lax.all_gather(down_hot, 'ep', axis=1, tiled=True)  66.8 us
    reduce_scatter x1, waiting for transfers between devices, body(): lax.psum_scatter(shadow_up.astype(jnp.bfloat16), 'ep', scatter_dimension=...  57.6 us
    psum x1, waiting for transfers between devices, body(): lax.psum(part_up_hot.astype(jnp.bfloat16), 'grp').astype(jnp.float32)  27.8 us
    psum x1, waiting for transfers between devices, body(): lax.psum(part_up.astype(jnp.bfloat16), 'grp').astype(jnp.float32)  26.7 us
    all_to_all x1, waiting for transfers between devices, body(): lax.all_to_all(outgoing[1], 'ep', split_axis=0, concat_axis=0, tiled=True)  13.3 us
  transfers between devices with their start and end apart: 12, of which 11 were waited for; matrix products, arithmetic and copies ran while one was open for 10% of the time, Pallas kernels for 0%

commit v1 on v0

--- a/solution.py
+++ b/solution.py
@@ -118,7 +118,13 @@
         lax.all_gather(gate_hot, "ep", axis=2, tiled=True),
         lax.all_gather(up_hot, "ep", axis=2, tiled=True),
     )
-    full_down = lax.all_gather(down_hot, "ep", axis=1, tiled=True)
+    devices = lax.axis_size("ep")
+    held, blocks = (down_hot, [down_hot])
+    for _ in range(devices - 1):
+        held = lax.ppermute(held, "ep", [(i, (i + 1) % devices) for i in range(devices)])
+        blocks.insert(0, held)
+    merged = jnp.concatenate(blocks, axis=1)
+    full_down = jnp.roll(merged, (lax.axis_index("ep") + 1) * down_hot.shape[1], axis=1)
     hot_weighted = (
         hot_scale.astype(jnp.float32)[:, :, None] * hot_cotan.astype(jnp.float32)
     ).astype(jnp.bfloat16)

time: 576 us -> 556 us (0.965)
  waiting for transfers between devices: 464 us -> 408 us
  starting transfers between devices: 24.6 us -> 40.4 us
  local copies, waits for them, and re-layouts: 11.6 us -> 22.1 us
  matrix products: 41.6 us -> 49.5 us
    ppermute x0 -> x7, waiting for transfers between devices: none -> 85.2 us  [body(): lax.ppermute(held, 'ep', [(i, (i + 1) % devices) for i in range(devices)])]
    all_gather x1 -> x0, waiting for transfers between devices: 66.8 us -> none  [body(): full_down = lax.all_gather(down_hot, 'ep', axis=1, tiled=True)]
    all_gather x1, waiting for transfers between devices: 67.5 us -> 21.6 us  [body(): lax.all_gather(up_hot, 'ep', axis=2, tiled=True)]
    unnamed x23 -> x40, local copies, waits for them, and re-layouts: 3.04 us -> 18.5 us
    all_gather x1, waiting for transfers between devices: 12.9 us -> 0.01 us  [body(): lax.all_gather(gate_hot, 'ep', axis=2, tiled=True)]
    all_to_all x1, waiting for transfers between devices: 13.3 us -> 4.56 us  [body(): lax.all_to_all(outgoing[1], 'ep', split_axis=0, concat_axis=0, tiled=True)]
    all_to_all x1, starting transfers between devices: 4.96 us -> 12.7 us  [body(): lax.all_to_all(outgoing[1], 'ep', split_axis=0, concat_axis=0, tiled=True)]
  transfers between devices with their start and end apart: 12 -> 18, of which waited for: 11 -> 15; matrix products, arithmetic and copies ran while one was open for 10% -> 13% of each run, Pallas kernels for 0% -> 0%
where the time goes in v1:
time: 556 us; the launch traced here: 554 us
  waiting for transfers between devices  408 us (73%)
  matrix products  49.5 us (9%)
  starting transfers between devices  40.4 us (7%)
  local copies, waits for them, and re-layouts  22.1 us (4%)
  between operations  14.5 us (3%)
  other arithmetic  12.9 us (2%)
  blocking collectives  6.71 us (1%)
    reduce_scatter x1, waiting for transfers between devices, body(): lax.psum_scatter(shadow_gate.astype(jnp.bfloat16), 'ep', scatter_dimensio...  86.1 us
    reduce_scatter x1, waiting for transfers between devices, body(): lax.psum_scatter(shadow_down.astype(jnp.bfloat16), 'ep', scatter_dimensio...  85.5 us
    ppermute x7, waiting for transfers between devices, body(): lax.ppermute(held, 'ep', [(i, (i + 1) % devices) for i in range(devices)])  85.2 us
    reduce_scatter x1, waiting for transfers between devices, body(): lax.psum_scatter(shadow_up.astype(jnp.bfloat16), 'ep', scatter_dimension=...  52.9 us
    psum x1, waiting for transfers between devices, body(): lax.psum(part_up_hot.astype(jnp.bfloat16), 'grp').astype(jnp.float32)  26.9 us
    psum x1, waiting for transfers between devices, body(): lax.psum(part_up.astype(jnp.bfloat16), 'grp').astype(jnp.float32)  26.8 us
    all_gather x1, waiting for transfers between devices, body(): lax.all_gather(up_hot, 'ep', axis=2, tiled=True)  21.6 us
    unnamed x40, local copies, waits for them, and re-layouts  18.5 us
  transfers between devices with their start and end apart: 18, of which 15 were waited for; matrix products, arithmetic and copies ran while one was open for 13% of the time, Pallas kernels for 0%

profile of v1, /device:TPU:0, one launch (start us, length us, event | category | flops | bytes accessed | tf_op | source)
XLA Modules:
  0.0 554.3 jit_solution(14156549120937686049)
XLA Ops:
  16.9 4.9 all-to-all-start.1
  28.1 24.1 %collective-permute-done.1 = bf16[2,96,1280]{2,1,0:T(8,128)(2,1)S(1)} collective-permute-done((bf16[2,96,1280]{2,1,0:T(8,128)(2,1)S(1)}, bf16[2,96,1280]{2,1,0:T(8,128)(2,1)S(1)}, u32[]{:S(2)}, u32[]{:S(2)}) %collective-permute-start.1) | collective-permute-done | bytes 491552 | tf_op jit(solution)/shard_map/ppermute | solution.py:124
  52.8 22.6 %collective-permute-done.2 = bf16[2,96,1280]{2,1,0:T(8,128)(2,1)} collective-permute-done((bf16[2,96,1280]{2,1,0:T(8,128)(2,1)S(1)}, bf16[2,96,1280]{2,1,0:T(8,128)(2,1)}, u32[]{:S(2)}, u32[]{:S(2)}) %collective-permute-start.2) | collective-permute-done | bytes 491552 | tf_op jit(solution)/shard_map/ppermute | solution.py:124
  79.5 21.7 %collective-permute-done.3 = bf16[2,96,1280]{2,1,0:T(8,128)(2,1)} collective-permute-done((bf16[2,96,1280]{2,1,0:T(8,128)(2,1)}, bf16[2,96,1280]{2,1,0:T(8,128)(2,1)}, u32[]{:S(2)}, u32[]{:S(2)}) %collective-permute-start.3) | collective-permute-done | bytes 491552 | tf_op jit(solution)/shard_map/ppermute | solution.py:124
  102.5 11.5 %all-to-all-start = ((bf16[8,16,1280]{2,1,0:T(8,128)(2,1)}), bf16[8,16,1280]{2,1,0:T(8,128)(2,1)S(1)}, u32[]{:S(2)}, u32[]{:S(2)}) async-start(bf16[8,16,1280]{2,1,0:T(8,128)(2,1)} %bitcast.119), calls=%async_computation | async-start | bytes 655360 | tf_op jit(solution)/shard_map/all_to_all | solution.py:79
  116.3 6.1 %collective-permute-done.4 = bf16[2,96,1280]{2,1,0:T(8,128)(2,1)} collective-permute-done((bf16[2,96,1280]{2,1,0:T(8,128)(2,1)}, bf16[2,96,1280]{2,1,0:T(8,128)(2,1)}, u32[]{:S(2)}, u32[]{:S(2)}) %collective-permute-start.4) | collective-permute-done | bytes 491552 | tf_op jit(solution)/shard_map/ppermute | solution.py:124
  122.4 11.0 %all-to-all-done = bf16[8,16,1280]{2,1,0:T(8,128)(2,1)S(1)} async-done(((bf16[8,16,1280]{2,1,0:T(8,128)(2,1)}), bf16[8,16,1280]{2,1,0:T(8,128)(2,1)S(1)}, u32[]{:S(2)}, u32[]{:S(2)}) %all-to-all-start) | async-done | bytes 327712 | tf_op jit(solution)/shard_map/all_to_all | solution.py:79
  133.4 12.7 %all-to-all-start.2 = ((bf16[8,16,1280]{2,1,0:T(8,128)(2,1)}), bf16[8,16,1280]{2,1,0:T(8,128)(2,1)S(1)}, u32[]{:S(2)}, u32[]{:S(2)}) async-start(bf16[8,16,1280]{2,1,0:T(8,128)(2,1)} %bitcast.120), calls=%async_computation.2 | async-start | bytes 655360 | tf_op jit(solution)/shard_map/all_to_all | solution.py:80
  153.6 4.6 all-to-all-done.2
  159.0 7.7 %collective-permute-done.6 = bf16[2,96,1280]{2,1,0:T(8,128)(2,1)} collective-permute-done((bf16[2,96,1280]{2,1,0:T(8,128)(2,1)}, bf16[2,96,1280]{2,1,0:T(8,128)(2,1)}, u32[]{:S(2)}, u32[]{:S(2)}) %collective-permute-start.6) | collective-permute-done | bytes 491552 | tf_op jit(solution)/shard_map/ppermute | solution.py:124
  184.6 3.9 convolution_convert_fusion.10
  188.5 21.6 %all-gather.3.cloned.1.call-done = bf16[2,1280,768]{1,2,0:T(8,128)(2,1)} async-done(((bf16[2,1280,96]{1,2,0:T(8,128)(2,1)}), bf16[2,1280,768]{1,2,0:T(8,128)(2,1)}) %all-gather.3.cloned.1.call-update) | async-done | bytes 3932176 | tf_op jit(solution)/shard_map/all_gather | solution.py:119
  210.1 3.9 convolution_convert_fusion.11
  216.6 26.9 %all-reduce.6.cloned.1.call-done = (bf16[2,16,768]{2,1,0:T(8,128)(2,1)}, bf16[2,16,768]{2,1,0:T(8,128)(2,1)}, bf16[2,16,768]{2,1,0:T(8,128)(2,1)}) async-done(((bf16[2,16,768]{2,1,0:T(8,128)(2,1)}, bf16[2,16,768]{2,1,0:T(8,128)(2,1)}, bf16[2,16,768]{2,1,0:T(8,128)(2,1)}), (bf16[2,16,768]{2,1,0:T(8,128)(2,1)}, bf16[2,16,768]{2,1,0:T(8,128)(2,1)}, bf16[2,16,768]{2,1,0:T(8,128)(2,1)})) %all-reduce.6.cloned.1.call-update) | async-done | bytes 147472 | tf_op jit(solution)/shard_map/psum | solution.py:140
  243.4 4.1 convolution_convert_fusion.1
  247.6 3.2 convolution_convert_fusion
  254.5 26.8 %all-reduce.8.cloned.1.call-done = (bf16[128,768]{1,0:T(8,128)(2,1)}, bf16[128,768]{1,0:T(8,128)(2,1)}, bf16[128,768]{1,0:T(8,128)(2,1)}) async-done(((bf16[128,768]{1,0:T(8,128)(2,1)}, bf16[128,768]{1,0:T(8,128)(2,1)}, bf16[128,768]{1,0:T(8,128)(2,1)}), (bf16[128,768]{1,0:T(8,128)(2,1)}, bf16[128,768]{1,0:T(8,128)(2,1)}, bf16[128,768]{1,0:T(8,128)(2,1)})) %all-reduce.8.cloned.1.call-update) | async-done | bytes 589840 | tf_op jit(solution)/shard_map/psum | solution.py:98
  292.0 3.3 fusion.29
  295.5 6.7 %all-reduce = (f32[8,1,16]{2,0,1:T(8,128)}, f32[32]{0:T(128)S(1)}) all-reduce(f32[8,1,16]{2,0,1:T(8,128)S(1)} %all_to_all.22, f32[32]{0:T(128)S(1)} %reshape.191), channel_id=1, replica_groups=mesh['grp'=4,'ep'=8] {'grp'}, use_global_device_ids=true, to_apply=%region_22.23 | all-reduce | flops 160 | bytes 1280 | tf_op jit(solution)/shard_map/psum | solution.py:169
  302.2 5.8 %all-to-all-start.3 = ((f32[8,1,16]{2,1,0:T(1,128)}), f32[8,1,16]{2,1,0:T(1,128)S(1)}, u32[]{:S(2)}, u32[]{:S(2)}) async-start(f32[8,1,16]{2,1,0:T(1,128)} %bitcast.19), calls=%async_computation.6 | async-start | bytes 8192 | tf_op jit(solution)/shard_map/all_to_all | solution.py:170
  308.1 6.2 %all-to-all-done.3 = f32[8,1,16]{2,1,0:T(1,128)S(1)} async-done(((f32[8,1,16]{2,1,0:T(1,128)}), f32[8,1,16]{2,1,0:T(1,128)S(1)}, u32[]{:S(2)}, u32[]{:S(2)}) %all-to-all-start.3) | async-done | bytes 544 | tf_op jit(solution)/shard_map/all_to_all | solution.py:170
  316.8 52.9 %reduce-scatter.6.cloned.1.call-done = bf16[2,1280,96]{1,2,0:T(8,128)(2,1)} async-done(((bf16[2,1280,768]{1,2,0:T(8,128)(2,1)}), bf16[2,1280,96]{1,2,0:T(8,128)(2,1)}) %reduce-scatter.6.cloned.1.call-update) | async-done | bytes 491536 | tf_op jit(solution)/shard_map/reduce_scatter | solution.py:161
  371.7 85.5 %reduce-scatter.8.cloned.1.call-done = bf16[2,1280,96]{1,2,0:T(8,128)(2,1)} async-done(((bf16[2,1280,768]{1,2,0:T(8,128)(2,1)}), bf16[2,1280,96]{1,2,0:T(8,128)(2,1)}) %reduce-scatter.8.cloned.1.call-update) | async-done | bytes 491536 | tf_op jit(solution)/shard_map/reduce_scatter | solution.py:164
  459.3 86.1 %reduce-scatter.4.cloned.1.call-done = bf16[2,1280,96]{1,2,0:T(8,128)(2,1)} async-done(((bf16[2,1280,768]{1,2,0:T(8,128)(2,1)}), bf16[2,1280,96]{1,2,0:T(8,128)(2,1)}) %reduce-scatter.4.cloned.1.call-update) | async-done | bytes 491536 | tf_op jit(solution)/shard_map/reduce_scatter | solution.py:158
  (128 shorter events, 76.2 us)
Async XLA Ops:
  7.2 206.9 %copy-start = (bf16[1,768,1280]{2,1,0:T(8,128)(2,1)S(1)}, bf16[1,768,1280]{2,1,0:T(8,128)(2,1)}, u32[]{:S(2)}) copy-start(bf16[1,768,1280]{2,1,0:T(8,128)(2,1)} %param.18) | copy-start | bytes 5898244
  7.2 177.5 %all-gather.5.cloned.1.call-start = ((), (), s32[]{:S(2)}) async-start(), calls=%async_computation.8 | async-start | bytes 4423680 | tf_op jit(solution)/shard_map/all_gather | solution.py:118
  7.9 17.6 %collective-permute-start = (bf16[2,96,1280]{2,1,0:T(8,128)(2,1)}, bf16[2,96,1280]{2,1,0:T(8,128)(2,1)S(1)}, u32[]{:S(2)}, u32[]{:S(2)}) collective-permute-start(bf16[2,96,1280]{2,1,0:T(8,128)(2,1)} %param.21), channel_id=1, source_target_pairs={{0,1},{1,2},{2,3},{3,4},{4,5},{5,6},{6,7},{7,0},{8,9},{9,10},{10,1... | collective-permute-start | bytes 1474568 | tf_op jit(solution)/shard_map/ppermute | solution.py:124
  16.9 85.6 %all-to-all-start.1 = ((bf16[8,1,16]{2,1,0:T(2,128)(2,1)}), bf16[8,1,16]{2,1,0:T(2,128)(2,1)S(1)}, u32[]{:S(2)}, u32[]{:S(2)}) async-start(bf16[8,1,16]{2,1,0:T(2,128)(2,1)} %all_to_all.24), calls=%async_computation.1 | async-start | bytes 8192 | tf_op jit(solution)/shard_map/all_to_all | solution.py:81
  21.8 188.3 %all-gather.3.cloned.1.call-start = ((), (), s32[]{:S(2)}) async-start(), calls=%async_computation.7 | async-start | bytes 4423680 | tf_op jit(solution)/shard_map/all_gather | solution.py:119
  25.5 49.9 %copy-start.3 = (bf16[2,96,1280]{2,1,0:T(8,128)(2,1)}, bf16[2,96,1280]{2,1,0:T(8,128)(2,1)S(1)}, u32[]{:S(2)}) copy-start(bf16[2,96,1280]{2,1,0:T(8,128)(2,1)S(1)} %collective-permute-done) | copy-start | bytes 1474564
  25.5 26.7 %collective-permute-start.1 = (bf16[2,96,1280]{2,1,0:T(8,128)(2,1)S(1)}, bf16[2,96,1280]{2,1,0:T(8,128)(2,1)S(1)}, u32[]{:S(2)}, u32[]{:S(2)}) collective-permute-start(bf16[2,96,1280]{2,1,0:T(8,128)(2,1)S(1)} %collective-permute-done), channel_id=1, source_target_pairs={{0,1},{1,2},{2,3},{3,4},{4,5},{5,6},{6,7},{7,0},{8,9},{9,10},{10,1... | collective-permute-start | bytes 1474568 | tf_op jit(solution)/shard_map/ppermute | solution.py:124
  52.2 25.2 %copy-start.5 = (bf16[2,96,1280]{2,1,0:T(8,128)(2,1)}, bf16[2,96,1280]{2,1,0:T(8,128)(2,1)S(1)}, u32[]{:S(2)}) copy-start(bf16[2,96,1280]{2,1,0:T(8,128)(2,1)S(1)} %collective-permute-done.1) | copy-start | bytes 1474564
  52.2 23.2 %collective-permute-start.2 = (bf16[2,96,1280]{2,1,0:T(8,128)(2,1)S(1)}, bf16[2,96,1280]{2,1,0:T(8,128)(2,1)}, u32[]{:S(2)}, u32[]{:S(2)}) collective-permute-start(bf16[2,96,1280]{2,1,0:T(8,128)(2,1)S(1)} %collective-permute-done.1), channel_id=1, source_target_pairs={{0,1},{1,2},{2,3},{3,4},{4,5},{5,6},{6,7},{7,0},{8,9},{9,10},{10,1... | collective-permute-start | bytes 1474568 | tf_op jit(solution)/shard_map/ppermute | solution.py:124
  75.4 25.7 %collective-permute-start.3 = (bf16[2,96,1280]{2,1,0:T(8,128)(2,1)}, bf16[2,96,1280]{2,1,0:T(8,128)(2,1)}, u32[]{:S(2)}, u32[]{:S(2)}) collective-permute-start(bf16[2,96,1280]{2,1,0:T(8,128)(2,1)} %collective-permute-done.2), channel_id=1, source_target_pairs={{0,1},{1,2},{2,3},{3,4},{4,5},{5,6},{6,7},{7,0},{8,9},{9,10},{10,1... | collective-permute-start | bytes 1474568 | tf_op jit(solution)/shard_map/ppermute | solution.py:124
  79.5 94.8 %copy-start.2 = (bf16[2,96,1280]{2,1,0:T(8,128)(2,1)S(1)}, bf16[2,96,1280]{2,1,0:T(8,128)(2,1)}, u32[]{:S(2)}) copy-start(bf16[2,96,1280]{2,1,0:T(8,128)(2,1)} %param.21) | copy-start | bytes 1474564
  101.2 21.2 %collective-permute-start.4 = (bf16[2,96,1280]{2,1,0:T(8,128)(2,1)}, bf16[2,96,1280]{2,1,0:T(8,128)(2,1)}, u32[]{:S(2)}, u32[]{:S(2)}) collective-permute-start(bf16[2,96,1280]{2,1,0:T(8,128)(2,1)} %collective-permute-done.3), channel_id=1, source_target_pairs={{0,1},{1,2},{2,3},{3,4},{4,5},{5,6},{6,7},{7,0},{8,9},{9,10},{10,1... | collective-permute-start | bytes 1474568 | tf_op jit(solution)/shard_map/ppermute | solution.py:124
  102.5 30.9 %all-to-all-start = ((bf16[8,16,1280]{2,1,0:T(8,128)(2,1)}), bf16[8,16,1280]{2,1,0:T(8,128)(2,1)S(1)}, u32[]{:S(2)}, u32[]{:S(2)}) async-start(bf16[8,16,1280]{2,1,0:T(8,128)(2,1)} %bitcast.119), calls=%async_computation | async-start | bytes 655360 | tf_op jit(solution)/shard_map/all_to_all | solution.py:79
  122.4 26.4 %collective-permute-start.5 = (bf16[2,96,1280]{2,1,0:T(8,128)(2,1)}, bf16[2,96,1280]{2,1,0:T(8,128)(2,1)}, u32[]{:S(2)}, u32[]{:S(2)}) collective-permute-start(bf16[2,96,1280]{2,1,0:T(8,128)(2,1)} %collective-permute-done.4), channel_id=1, source_target_pairs={{0,1},{1,2},{2,3},{3,4},{4,5},{5,6},{6,7},{7,0},{8,9},{9,10},{10,1... | collective-permute-start | bytes 1474568 | tf_op jit(solution)/shard_map/ppermute | solution.py:124
  133.4 24.8 %all-to-all-start.2 = ((bf16[8,16,1280]{2,1,0:T(8,128)(2,1)}), bf16[8,16,1280]{2,1,0:T(8,128)(2,1)S(1)}, u32[]{:S(2)}, u32[]{:S(2)}) async-start(bf16[8,16,1280]{2,1,0:T(8,128)(2,1)} %bitcast.120), calls=%async_computation.2 | async-start | bytes 655360 | tf_op jit(solution)/shard_map/all_to_all | solution.py:80
  146.1 97.4 %all-reduce.6.cloned.1.call-start = ((), (), s32[]{:S(2)}) async-start(), calls=%async_computation.12 | async-start | bytes 294912 | tf_op jit(solution)/shard_map/psum | solution.py:140
  148.8 17.9 %collective-permute-start.6 = (bf16[2,96,1280]{2,1,0:T(8,128)(2,1)}, bf16[2,96,1280]{2,1,0:T(8,128)(2,1)}, u32[]{:S(2)}, u32[]{:S(2)}) collective-permute-start(bf16[2,96,1280]{2,1,0:T(8,128)(2,1)} %collective-permute-done.5), channel_id=1, source_target_pairs={{0,1},{1,2},{2,3},{3,4},{4,5},{5,6},{6,7},{7,0},{8,9},{9,10},{10,1... | collective-permute-start | bytes 1474568 | tf_op jit(solution)/shard_map/ppermute | solution.py:124
  158.1 21.5 %copy-start.6 = (bf16[2,96,1280]{2,1,0:T(8,128)(2,1)S(1)}, bf16[2,96,1280]{2,1,0:T(8,128)(2,1)}, u32[]{:S(2)}) copy-start(bf16[2,96,1280]{2,1,0:T(8,128)(2,1)} %copy-done.5) | copy-start | bytes 1474564
  158.1 21.6 %copy-start.4 = (bf16[2,96,1280]{2,1,0:T(8,128)(2,1)S(1)}, bf16[2,96,1280]{2,1,0:T(8,128)(2,1)}, u32[]{:S(2)}) copy-start(bf16[2,96,1280]{2,1,0:T(8,128)(2,1)} %copy-done.3) | copy-start | bytes 1474564
  214.0 67.3 %all-reduce.8.cloned.1.call-start = ((), (), s32[]{:S(2)}) async-start(), calls=%async_computation.13 | async-start | bytes 1179648 | tf_op jit(solution)/shard_map/psum | solution.py:98
  216.5 153.2 %reduce-scatter.6.cloned.1.call-start = ((), (), s32[]{:S(2)}) async-start(), calls=%async_computation.10 | async-start | bytes 4423680 | tf_op jit(solution)/shard_map/reduce_scatter | solution.py:161
  247.6 209.7 %reduce-scatter.8.cloned.1.call-start = ((), (), s32[]{:S(2)}) async-start(), calls=%async_computation.11 | async-start | bytes 4423680 | tf_op jit(solution)/shard_map/reduce_scatter | solution.py:164
  250.9 294.6 %reduce-scatter.4.cloned.1.call-start = ((), (), s32[]{:S(2)}) async-start(), calls=%async_computation.9 | async-start | bytes 4423680 | tf_op jit(solution)/shard_map/reduce_scatter | solution.py:158
  302.2 12.2 %all-to-all-start.3 = ((f32[8,1,16]{2,1,0:T(1,128)}), f32[8,1,16]{2,1,0:T(1,128)S(1)}, u32[]{:S(2)}, u32[]{:S(2)}) async-start(f32[8,1,16]{2,1,0:T(1,128)} %bitcast.19), calls=%async_computation.6 | async-start | bytes 8192 | tf_op jit(solution)/shard_map/all_to_all | solution.py:170
  (5 other events, 26.9 us)
Sparse Core Ops, SparseCore 0:
  10.2 98.9 all-gather.4
  111.4 98.6 all-gather.2
  214.1 29.2 all-reduce.5
  246.6 34.6 all-reduce.7
  285.2 84.4 reduce-scatter.5
  373.2 83.9 reduce-scatter.7
  461.4 83.9 reduce-scatter.3
